TPU v7x, 32 devices: a whole 2x2x4 slice. The times are simulated.
32 devices in a mesh: leaf: 8 (over z, y), blk: 4 (over x, core).
Axes of the slice: x: 2, y: 2, z: 4, core: 2. Of those that a mesh axis runs over, the one named last changes fastest.
Arguments:
- parent_inverse: bfloat16 [8, 512, 512], P('leaf', None, 'blk'), as said below
- leaf_inverse: bfloat16 [112, 512, 512], P('leaf', 'blk'), as said below
- coupling: bfloat16 [112, 512, 512], P('leaf', 'blk'), may hold values from -0.25 to 0.25
- sensitivity: bfloat16 [112, 512, 512], P('leaf', 'blk'), may hold values from -0.25 to 0.25
- parent_of: int32 [112, 1], P('leaf'), may hold values from 0 to 7
- leaf_field: bfloat16 [112, 512], P('leaf'), may hold values from -6 to 6
- parent_field: bfloat16 [8, 512], P('leaf', 'blk'), may hold values from -6 to 6
Outputs:
- leaf_grad: float32 [112, 512], P('leaf', 'blk')
- coupling_grad: float32 [8, 512], P('leaf', 'blk')
Inputs may be any that keep to these rules, and one draw needn't show every extreme that they name: `parent_of`: every one of the 8 separator supernodes is the parent of at least one leaf. `parent_inverse`: lower triangular with a positive diagonal. `leaf_inverse`: lower triangular with a positive diagonal.
All inputs are finite; a program needn't handle non-finite values.
Results may differ from a plain program's by a relative error of at most 0.0006.
Values may be sent and summed in bfloat16 or wider, within the bound.
No kernel may reach another device: no remote copies, remote signals or barrier semaphores. Data moves between devices by JAX's collectives and lax.ppermute only.
A program may use at most 128 MiB of HBM per device.

v0:
```python
import jax
import jax.numpy as jnp
from jax import lax
from jax.sharding import PartitionSpec as P


def body(parent_inverse, leaf_inverse, coupling, sensitivity, parent_of, leaf_field, parent_field):
    count = coupling.shape[0]
    share = coupling.shape[1]
    width = coupling.shape[2]
    offset = lax.axis_index("blk") * share
    cov_rows = jnp.einsum(
        "pkr,pkc->prc",
        parent_inverse,
        lax.all_gather(parent_inverse, "blk", axis=2, tiled=True),
        preferred_element_type=jnp.float32,
    ).astype(jnp.bfloat16)
    parent_ids = parent_of[:, 0]
    initial = (
        jnp.zeros((count, share, width), jnp.bfloat16),
        jnp.zeros((count, share), jnp.bfloat16),
    )
    pieces = (
        lax.all_gather(cov_rows, "leaf", axis=0, tiled=True),
        lax.all_gather(parent_field, "leaf", axis=0, tiled=True),
    )
    number = pieces[0].shape[0]
    inside = (parent_ids >= 0) & (parent_ids < number)
    position = jnp.clip(parent_ids, 0, number - 1)
    taken_cov = jnp.take(pieces[0], position, axis=0)
    taken_field = jnp.take(pieces[1], position, axis=0)
    chosen_cov = jnp.where(inside[:, None, None], taken_cov, initial[0])
    chosen_field = jnp.where(inside[:, None], taken_field, initial[1])
    panel = coupling
    mixed = jnp.einsum(
        "lik,lkc->lic",
        panel,
        lax.all_gather(leaf_inverse, "blk", axis=1, tiled=True),
        preferred_element_type=jnp.float32,
    ).astype(jnp.bfloat16)
    cross = jnp.zeros((count, share, width), jnp.float32) - jnp.einsum(
        "lrk,lkc->lrc",
        chosen_cov,
        lax.all_gather(mixed, "blk", axis=1, tiled=True),
        preferred_element_type=jnp.float32,
    )
    cross_half = cross.astype(jnp.bfloat16)
    panel = coupling
    update = lax.psum_scatter(
        jnp.einsum("lik,lia->kla", panel, cross_half, preferred_element_type=jnp.float32),
        "blk",
        scatter_dimension=0,
        tiled=True,
    )
    factor = leaf_inverse.astype(jnp.float32)
    partial_diag = jnp.sum(factor * factor, 1) - jnp.einsum(
        "lka,kla->la", factor, update, precision=lax.Precision.HIGHEST
    )
    diagonal = lax.psum_scatter(partial_diag, "blk", scatter_dimension=1, tiled=True)
    value = lax.dynamic_slice_in_dim(leaf_field, offset, share, 1).astype(jnp.float32)
    leaf_grad = 0.5 * (diagonal - value * value)
    returned = jnp.sum(sensitivity.astype(jnp.float32) * cross, 2) - chosen_field.astype(
        jnp.float32
    ) * jnp.einsum("lab,lb->la", sensitivity, leaf_field, preferred_element_type=jnp.float32)
    parent_total = lax.axis_size("leaf")
    owners = (
        parent_ids[:, None] == lax.broadcasted_iota(jnp.int32, (count, parent_total), 1)
    ).astype(jnp.float32)
    spread = jnp.einsum("lp,la->pa", owners, returned, precision=lax.Precision.HIGHEST)
    coupling_grad = lax.psum_scatter(spread, "leaf", scatter_dimension=0, tiled=True)
    return (leaf_grad, coupling_grad)


def solution(mesh):
    in_specs = (
        P("leaf", None, "blk"),
        P("leaf", "blk", None),
        P("leaf", "blk", None),
        P("leaf", "blk", None),
        P("leaf", None),
        P("leaf", None),
        P("leaf", "blk"),
    )
    out_specs = (P("leaf", "blk"), P("leaf", "blk"))
    return jax.shard_map(body, mesh=mesh, in_specs=in_specs, out_specs=out_specs, check_vma=False)
```

profile of v0, /device:TPU:0, one launch (start us, length us, event | category | flops | bytes accessed | tf_op | source)
XLA Modules:
  0.0 319.3 jit_solution(10498825598781214529)
XLA Ops:
  7.2 0.7 all-gather.6.cloned.1.call-update
  8.2 8.6 %all_gather.15 = bf16[1,512,512]{2,1,0:T(8,128)(2,1)S(1)} all-gather(bf16[1,512,128]{2,1,0:T(8,128)(2,1)S(1)} %copy-done.2), channel_id=1, replica_groups=mesh['leaf'=8,'blk'=4] {'blk'}, dimensions={2}, use_global_device_ids=true | all-gather | bytes 655360 | tf_op jit(solution)/shard_map/all_gather | solution.py:15
  16.9 0.9 convolution_convert_fusion.1
  17.8 46.8 %all-gather.6.cloned.1.call-done = bf16[14,512,512]{2,1,0:T(8,128)(2,1)} async-done(((bf16[14,128,512]{2,1,0:T(8,128)(2,1)}), bf16[14,512,512]{2,1,0:T(8,128)(2,1)}) %all-gather.6.cloned.1.call-update) | async-done | bytes 7340048 | tf_op jit(solution)/shard_map/all_gather | solution.py:38
  64.7 5.5 %convolution_convert_fusion = bf16[14,128,512]{2,1,0:T(8,128)(2,1)} fusion(bf16[14,128,512]{2,1,0:T(8,128)(2,1)S(1)} %copy-done, bf16[14,512,512]{2,1,0:T(8,128)(2,1)} %all-gather.6.cloned.1.call-done), kind=kOutput, calls=%fused_computation.13 | convolution fusion | flops 940441600 | bytes 11010048 | tf_op jit(solution)/shard_map/lik,lkc->lic/dot_general | solution.py:35
  70.3 0.6 copy-done.5
  70.9 36.3 %all-gather.10.cloned.1.call-done = bf16[1024,512]{1,0:T(8,128)(2,1)} async-done(((bf16[128,512]{1,0:T(8,128)(2,1)}), bf16[1024,512]{1,0:T(8,128)(2,1)}) %all-gather.10.cloned.1.call-update) | async-done | bytes 1048592 | tf_op jit(solution)/shard_map/all_gather | solution.py:24
  107.2 3.2 gather_fusion
  110.4 49.5 %all-gather.8.cloned.1.call-done = bf16[14,512,512]{2,1,0:T(8,128)(2,1)} async-done(((bf16[14,128,512]{2,1,0:T(8,128)(2,1)}), bf16[14,512,512]{2,1,0:T(8,128)(2,1)}) %all-gather.8.cloned.1.call-update) | async-done | bytes 7340048 | tf_op jit(solution)/shard_map/all_gather | solution.py:44
  159.8 5.4 %multiply_reduce_fusion.1 = (f32[14,128]{1,0:T(8,128)S(1)}, f32[14,128,512]{2,1,0:T(8,128)S(1)}) fusion(bf16[14,128,512]{2,1,0:T(8,128)(2,1)} %param.10, bf16[14,512,512]{2,1,0:T(8,128)(2,1)} %all-gather.8.cloned.1.call-done, bf16[14,128,512]{2,1,0:T(8,128)(2,1)} %gather_fusion, pred[14]{0:T(512)(128)(4,1)S(1)} %get-tuple-element.3, ...), kind=kOutput, calls=%fused_computation.4 | convolution fusion | flops 945027328 | bytes 14687260 | tf_op jit(solution)/shard_map/lrk,lkc->lrc/dot_general | solution.py:41
  165.2 7.3 %convolution_bitcast_fusion = f32[512,14,512]{0,2,1:T(8,128)} fusion(bf16[14,128,512]{2,1,0:T(8,128)(2,1)S(1)} %copy-done, f32[14,128,512]{2,1,0:T(8,128)S(1)} %get-tuple-element.5), kind=kOutput, calls=%fused_computation.2 | convolution fusion | flops 941359104 | bytes 20185088 | tf_op jit(solution)/shard_map/lik,lia->kla/dot_general | solution.py:50
  173.2 20.5 %all-gather.1 = bf16[8,1,128]{2,1,0:T(2,128)(2,1)S(1)} all-gather(bf16[1,1,128]{2,1,0:T(2,128)(2,1)S(1)} %bitcast.40), channel_id=1, replica_groups=mesh['leaf'=8,'blk'=4] {'leaf'}, dimensions={0}, use_global_device_ids=true | all-gather | bytes 2304 | tf_op jit(solution)/shard_map/all_gather | solution.py:25
  193.7 0.6 gather_fusion.1
  194.3 0.6 dynamic-slice
  194.9 1.9 multiply_reduce_fusion.2
  196.8 0.6 fusion.10
  197.7 17.3 %all-reduce = f32[8,128]{1,0:T(8,128)S(1)} all-reduce(f32[8,128]{1,0:T(8,128)S(1)} %fusion.13), channel_id=5, replica_groups=mesh['leaf'=8,'blk'=4] {'leaf'}, use_global_device_ids=true, to_apply=%region_4.5.clone | all-reduce | flops 1024 | bytes 8192
  214.9 67.8 %reduce-scatter.3.cloned.1.call-done = f32[128,14,512]{0,2,1:T(8,128)} async-done(((f32[512,14,512]{0,2,1:T(8,128)}), f32[128,14,512]{0,2,1:T(8,128)}) %reduce-scatter.3.cloned.1.call-update) | async-done | bytes 3670032 | tf_op jit(solution)/shard_map/reduce_scatter | solution.py:49
  282.8 5.1 %copy.17 = f32[14,512,128]{1,2,0:T(8,128)} copy(f32[14,512,128]{2,1,0:T(8,128)} %bitcast.36) | data formatting | bytes 7340032
  287.9 3.2 %multiply_reduce_fusion = f32[14,512]{1,0:T(8,128)S(1)} fusion(f32[14,512,128]{1,2,0:T(8,128)} %copy.17, bf16[14,128,512]{2,1,0:T(8,128)(2,1)} %param.8), kind=kLoop, calls=%fused_computation.3 | loop fusion | flops 2745344 | bytes 5533696 | tf_op jit(solution)/shard_map/lka,kla->la/dot_general | solution.py:56
  291.1 0.6 sub.13
  291.8 1.2 constant_dynamic-slice_fusion
  293.0 18.5 %reduce-scatter.5.cloned.1.call-done = f32[14,128]{1,0:T(8,128)} async-done(((f32[14,512]{1,0:T(8,128)}), f32[14,128]{1,0:T(8,128)}) %reduce-scatter.5.cloned.1.call-update) | async-done | bytes 7184 | tf_op jit(solution)/shard_map/reduce_scatter | solution.py:59
  311.5 1.3 subtract_multiply_fusion
  (28 shorter events, 1.4 us)
Async XLA Ops:
  7.2 57.5 %copy-start = (bf16[14,128,512]{2,1,0:T(8,128)(2,1)S(1)}, bf16[14,128,512]{2,1,0:T(8,128)(2,1)}, u32[]{:S(2)}) copy-start(bf16[14,128,512]{2,1,0:T(8,128)(2,1)} %param.9) | copy-start | bytes 5505028
  7.2 1.0 copy-start.2
  7.2 57.5 %all-gather.6.cloned.1.call-start = ((), (), s32[]{:S(2)}) async-start(), calls=%async_computation.2 | async-start | bytes 9175040 | tf_op jit(solution)/shard_map/all_gather | solution.py:38
  7.9 99.3 %all-gather.10.cloned.1.call-start = ((), (), s32[]{:S(2)}) async-start(), calls=%async_computation.6 | async-start | bytes 1179648 | tf_op jit(solution)/shard_map/all_gather | solution.py:24
  17.8 142.0 %all-gather.8.cloned.1.call-start = ((), (), s32[]{:S(2)}) async-start(), calls=%async_computation.3 | async-start | bytes 9175040 | tf_op jit(solution)/shard_map/all_gather | solution.py:44
  70.2 0.7 copy-start.5
  70.2 212.6 %reduce-scatter.3.cloned.1.call-start = ((), (), s32[]{:S(2)}) async-start(), calls=%async_computation.4 | async-start | bytes 18350080 | tf_op jit(solution)/shard_map/reduce_scatter | solution.py:49
  172.6 0.7 copy-start.4
  172.6 21.7 %copy-start.6 = (u32[32]{0:T(128)S(1)}, u32[32]{0:T(128)}, u32[]{:S(2)}) copy-start(u32[32]{0:T(128)} %constant.58) | copy-start | bytes 388
  172.6 24.2 %copy-start.3 = (bf16[14,512]{1,0:T(8,128)(2,1)S(1)}, bf16[14,512]{1,0:T(8,128)(2,1)}, u32[]{:S(2)}) copy-start(bf16[14,512]{1,0:T(8,128)(2,1)} %param.12) | copy-start | bytes 43012
  172.6 138.9 %reduce-scatter.5.cloned.1.call-start = ((), (), s32[]{:S(2)}) async-start(), calls=%async_computation.5 | async-start | bytes 40960 | tf_op jit(solution)/shard_map/reduce_scatter | solution.py:59
  194.3 2.5 copy-start.1
Sparse Core Ops, SparseCore 0:
  9.6 55.0 all-gather.5
  66.8 40.3 all-gather.9
  108.8 51.0 all-gather.7
  172.7 110.0 reduce-scatter.2
  291.9 19.5 reduce-scatter.4
where the time goes:
time: 320 us; the launch traced here: 319 us
  waiting for transfers between devices  220 us (69%)
  blocking collectives  46.4 us (14%)
  matrix products  20 us (6%)
  between operations  13.9 us (4%)
  local copies, waits for them, and re-layouts  12 us (4%)
  other arithmetic  7.09 us (2%)
    reduce_scatter x1, waiting for transfers between devices, body(): lax.psum_scatter(jnp.einsum('lik,lia->kla', panel, cross_half, preferred_...  67.8 us
    all_gather x1, waiting for transfers between devices, body(): lax.all_gather(mixed, 'blk', axis=1, tiled=True)  49.5 us
    all_gather x1, waiting for transfers between devices, body(): lax.all_gather(leaf_inverse, 'blk', axis=1, tiled=True)  46.8 us
    all_gather x1, waiting for transfers between devices, body(): lax.all_gather(cov_rows, 'leaf', axis=0, tiled=True)  36.3 us
    all_gather x1, blocking collectives, body(): lax.all_gather(parent_field, 'leaf', axis=0, tiled=True)  20.5 us
    reduce_scatter x1, waiting for transfers between devices, body(): lax.psum_scatter(partial_diag, 'blk', scatter_dimension=1, tiled=True)  18.5 us
    unnamed x1, blocking collectives  17.3 us
    all_gather x1, blocking collectives, body(): lax.all_gather(parent_inverse, 'blk', axis=2, tiled=True)  8.63 us
  transfers between devices with their start and end apart: 5, of which 5 were waited for; matrix products, arithmetic and copies ran while one was open for 5% of the time, Pallas kernels for 0%

commit v1 on v0

--- a/solution.py
+++ b/solution.py
@@ -38,11 +38,34 @@
         lax.all_gather(leaf_inverse, "blk", axis=1, tiled=True),
         preferred_element_type=jnp.float32,
     ).astype(jnp.bfloat16)
-    cross = jnp.zeros((count, share, width), jnp.float32) - jnp.einsum(
-        "lrk,lkc->lrc",
-        chosen_cov,
-        lax.all_gather(mixed, "blk", axis=1, tiled=True),
-        preferred_element_type=jnp.float32,
+
+    def attach_flows(field_in, along_dim, z):
+        mid_arr = lax.axis_size("blk")
+        mat_out, u_next, base_arr = (mid_arr, lax.axis_index("blk"), field_in.shape[along_dim])
+        pool = [(jj, (jj + 1) % mat_out) for jj in range(mat_out)]
+        views = [(jj, (jj - 1) % mat_out) for jj in range(mat_out)]
+        plain = mat_out // 2
+        z_new = x_next = field_in
+        lower = z(field_in, u_next * base_arr)
+        for w in range(1, plain + 1):
+            z_new = lax.ppermute(z_new, axis_name="blk", perm=pool)
+            if w < mat_out - plain:
+                x_next = lax.ppermute(x_next, axis_name="blk", perm=views)
+                side_arr = z(x_next, (u_next + w) % mat_out * base_arr)
+                lower = lower + side_arr
+            reached = z(z_new, (u_next - w) % mat_out * base_arr)
+            lower = lower + reached
+        return lower
+
+    cross = jnp.zeros((count, share, width), jnp.float32) - attach_flows(
+        mixed,
+        1,
+        lambda own_block, offset_2: jnp.einsum(
+            "lrk,lkc->lrc",
+            lax.dynamic_slice_in_dim(chosen_cov, offset_2, own_block.shape[1], axis=2),
+            own_block,
+            preferred_element_type=jnp.float32,
+        ),
     )
     cross_half = cross.astype(jnp.bfloat16)
     panel = coupling

time: 320 us -> 307 us (0.959)
  waiting for transfers between devices: 220 us -> 184 us
  blocking collectives: 46.4 us -> 62.1 us
  matrix products: 20 us -> 23.9 us
    all_gather x1 -> x0, waiting for transfers between devices: 49.5 us -> none  [body(): lax.all_gather(mixed, 'blk', axis=1, tiled=True)]
    all_gather x1, blocking collectives: 8.63 us -> 26 us  [body(): lax.all_gather(parent_inverse, 'blk', axis=2, tiled=True)]
    all_gather x1, waiting for transfers between devices: 46.8 us -> 56.6 us  [body(): lax.all_gather(leaf_inverse, 'blk', axis=1, tiled=True)]
    dot_general x1 -> x4, matrix products: 5.4 us -> 9.33 us  [body(): jnp.einsum('lrk,lkc->lrc', lax.dynamic_slice_in_dim(chosen_cov, offset_2,...]
    all_gather x1, waiting for transfers between devices: 36.3 us -> 39.7 us  [body(): lax.all_gather(cov_rows, 'leaf', axis=0, tiled=True)]
    unnamed x18 -> x20, local copies, waits for them, and re-layouts: 8.29 us -> 7.47 us
  transfers between devices with their start and end apart: 5 -> 7, of which waited for: 5 -> 4; matrix products, arithmetic and copies ran while one was open for 5% -> 6% of each run, Pallas kernels for 0% -> 0%
where the time goes in v1:
time: 307 us; the launch traced here: 306 us
  waiting for transfers between devices  184 us (60%)
  blocking collectives  62.1 us (20%)
  matrix products  23.9 us (8%)
  between operations  15.3 us (5%)
  local copies, waits for them, and re-layouts  11.2 us (4%)
  other arithmetic  8.85 us (3%)
    reduce_scatter x1, waiting for transfers between devices, body(): lax.psum_scatter(jnp.einsum('lik,lia->kla', panel, cross_half, preferred_...  68.2 us
    all_gather x1, waiting for transfers between devices, body(): lax.all_gather(leaf_inverse, 'blk', axis=1, tiled=True)  56.6 us
    all_gather x1, waiting for transfers between devices, body(): lax.all_gather(cov_rows, 'leaf', axis=0, tiled=True)  39.7 us
    all_gather x1, blocking collectives, body(): lax.all_gather(parent_inverse, 'blk', axis=2, tiled=True)  26 us
    reduce_scatter x1, waiting for transfers between devices, body(): lax.psum_scatter(partial_diag, 'blk', scatter_dimension=1, tiled=True)  18.5 us
    all_gather x1, blocking collectives, body(): lax.all_gather(parent_field, 'leaf', axis=0, tiled=True)  18.3 us
    unnamed x1, blocking collectives  17.8 us
    dot_general x4, matrix products, body(): jnp.einsum('lrk,lkc->lrc', lax.dynamic_slice_in_dim(chosen_cov, offset_2,...  9.33 us
  transfers between devices with their start and end apart: 7, of which 4 were waited for; matrix products, arithmetic and copies ran while one was open for 6% of the time, Pallas kernels for 0%

profile of v1, /device:TPU:0, one launch (start us, length us, event | category | flops | bytes accessed | tf_op | source)
XLA Modules:
  0.0 306.2 jit_solution(16177981464992754310)
XLA Ops:
  8.1 0.7 all-gather.5.cloned.1.call-update
  8.8 56.6 %all-gather.5.cloned.1.call-done = bf16[14,512,512]{2,1,0:T(8,128)(2,1)} async-done(((bf16[14,128,512]{2,1,0:T(8,128)(2,1)}), bf16[14,512,512]{2,1,0:T(8,128)(2,1)}) %all-gather.5.cloned.1.call-update) | async-done | bytes 7340048 | tf_op jit(solution)/shard_map/all_gather | solution.py:38
  65.4 5.5 %convolution_convert_fusion = bf16[14,128,512]{2,1,0:T(8,128)(2,1)} fusion(bf16[14,128,512]{2,1,0:T(8,128)(2,1)S(1)} %copy-done, bf16[14,512,512]{2,1,0:T(8,128)(2,1)} %all-gather.5.cloned.1.call-done), kind=kOutput, calls=%fused_computation.9 | convolution fusion | flops 940441600 | bytes 11010048 | tf_op jit(solution)/shard_map/lik,lkc->lic/dot_general | solution.py:35
  71.2 26.0 %all_gather.12 = bf16[1,512,512]{2,1,0:T(8,128)(2,1)S(1)} all-gather(bf16[1,512,128]{2,1,0:T(8,128)(2,1)S(1)} %copy-done.3), channel_id=1, replica_groups=mesh['leaf'=8,'blk'=4] {'blk'}, dimensions={2}, use_global_device_ids=true | all-gather | bytes 655360 | tf_op jit(solution)/shard_map/all_gather | solution.py:15
  97.2 0.9 convolution_convert_fusion.1
  98.8 39.7 %all-gather.7.cloned.1.call-done = bf16[1024,512]{1,0:T(8,128)(2,1)} async-done(((bf16[128,512]{1,0:T(8,128)(2,1)}), bf16[1024,512]{1,0:T(8,128)(2,1)}) %all-gather.7.cloned.1.call-update) | async-done | bytes 1048592 | tf_op jit(solution)/shard_map/all_gather | solution.py:24
  138.5 3.2 %gather_fusion = bf16[14,128,512]{2,1,0:T(8,128)(2,1)} fusion(bf16[8,128,512]{2,1,0:T(8,128)(2,1)} %bitcast.41, s32[1024]{0:T(1024)S(1)} %pad_clamp_fusion), kind=kCustom, calls=%fused_computation | custom fusion | bytes 3670072 | tf_op jit(solution)/shard_map/jit(_take)/gather | solution.py:30
  141.7 1.8 select_select_fusion
  143.5 2.1 fusion.7
  145.6 2.1 fusion.3
  147.8 2.3 fusion.5
  150.0 2.8 multiply_reduce_fusion.1
  152.9 7.3 %convolution_bitcast_fusion = f32[512,14,512]{0,2,1:T(8,128)} fusion(bf16[14,128,512]{2,1,0:T(8,128)(2,1)S(1)} %copy-done, bf16[14,128,512]{2,1,0:T(8,128)(2,1)S(1)} %get-tuple-element.5), kind=kOutput, calls=%fused_computation.2 | convolution fusion | flops 939524096 | bytes 18350080 | tf_op jit(solution)/shard_map/lik,lia->kla/dot_general | solution.py:73
  160.8 18.3 %all-gather.1 = bf16[8,1,128]{2,1,0:T(2,128)(2,1)S(1)} all-gather(bf16[1,1,128]{2,1,0:T(2,128)(2,1)S(1)} %bitcast.44), channel_id=1, replica_groups=mesh['leaf'=8,'blk'=4] {'leaf'}, dimensions={0}, use_global_device_ids=true | all-gather | bytes 2304 | tf_op jit(solution)/shard_map/all_gather | solution.py:25
  179.7 0.6 dynamic-slice
  180.3 1.9 multiply_reduce_fusion.2
  183.1 17.8 %all-reduce = f32[8,128]{1,0:T(8,128)S(1)} all-reduce(f32[8,128]{1,0:T(8,128)S(1)} %fusion.13), channel_id=5, replica_groups=mesh['leaf'=8,'blk'=4] {'leaf'}, use_global_device_ids=true, to_apply=%region_4.5.clone | all-reduce | flops 1024 | bytes 8192
  200.9 68.2 %reduce-scatter.3.cloned.1.call-done = f32[128,14,512]{0,2,1:T(8,128)} async-done(((f32[512,14,512]{0,2,1:T(8,128)}), f32[128,14,512]{0,2,1:T(8,128)}) %reduce-scatter.3.cloned.1.call-update) | async-done | bytes 3670032 | tf_op jit(solution)/shard_map/reduce_scatter | solution.py:72
  269.1 5.1 %copy.17 = f32[14,512,128]{1,2,0:T(8,128)} copy(f32[14,512,128]{2,1,0:T(8,128)} %bitcast.40) | data formatting | bytes 7340032
  274.2 3.2 %multiply_reduce_fusion = f32[14,512]{1,0:T(8,128)S(1)} fusion(f32[14,512,128]{1,2,0:T(8,128)} %copy.17, bf16[14,128,512]{2,1,0:T(8,128)(2,1)} %param.8), kind=kLoop, calls=%fused_computation.3 | loop fusion | flops 2745344 | bytes 5533696 | tf_op jit(solution)/shard_map/lka,kla->la/dot_general | solution.py:79
  277.5 0.6 sub.21
  278.1 1.2 constant_dynamic-slice_fusion
  279.3 18.5 %reduce-scatter.5.cloned.1.call-done = f32[14,128]{1,0:T(8,128)} async-done(((f32[14,512]{1,0:T(8,128)}), f32[14,128]{1,0:T(8,128)}) %reduce-scatter.5.cloned.1.call-update) | async-done | bytes 7184 | tf_op jit(solution)/shard_map/reduce_scatter | solution.py:82
  297.8 1.3 subtract_multiply_fusion
  (37 shorter events, 3.1 us)
Async XLA Ops:
  8.0 57.5 %copy-start = (bf16[14,128,512]{2,1,0:T(8,128)(2,1)S(1)}, bf16[14,128,512]{2,1,0:T(8,128)(2,1)}, u32[]{:S(2)}) copy-start(bf16[14,128,512]{2,1,0:T(8,128)(2,1)} %param.9) | copy-start | bytes 5505028
  8.0 57.4 %all-gather.5.cloned.1.call-start = ((), (), s32[]{:S(2)}) async-start(), calls=%async_computation.2 | async-start | bytes 9175040 | tf_op jit(solution)/shard_map/all_gather | solution.py:38
  8.7 62.5 %copy-start.3 = (bf16[1,512,128]{2,1,0:T(8,128)(2,1)S(1)}, bf16[1,512,128]{2,1,0:T(8,128)(2,1)}, u32[]{:S(2)}) copy-start(bf16[1,512,128]{2,1,0:T(8,128)(2,1)} %param.7) | copy-start | bytes 393220
  8.8 89.6 %copy-start.6 = (s32[14,1]{0,1:T(1,128)S(1)}, s32[14,1]{0,1:T(1,128)}, u32[]{:S(2)}) copy-start(s32[14,1]{0,1:T(1,128)} %param.11) | copy-start | bytes 172
  8.8 129.8 %all-gather.7.cloned.1.call-start = ((), (), s32[]{:S(2)}) async-start(), calls=%async_computation.5 | async-start | bytes 1179648 | tf_op jit(solution)/shard_map/all_gather | solution.py:24
  71.0 27.4 %collective-permute-start.1 = (bf16[14,128,512]{2,1,0:T(8,128)(2,1)}, bf16[14,128,512]{2,1,0:T(8,128)(2,1)}, u32[]{:S(2)}, u32[]{:S(2)}) collective-permute-start(bf16[14,128,512]{2,1,0:T(8,128)(2,1)} %convolution_convert_fusion), channel_id=1, source_target_pairs={{0,1},{1,2},{2,3},{3,0},{4,5},{5,6},{6,7},{7,4},{8,9},{9,10},{10,1... | collective-permute-start | bytes 5505032 | tf_op jit(solution)/shard_map/ppermute | solution.py:51
  98.1 171.0 %reduce-scatter.3.cloned.1.call-start = ((), (), s32[]{:S(2)}) async-start(), calls=%async_computation.3 | async-start | bytes 18350080 | tf_op jit(solution)/shard_map/reduce_scatter | solution.py:72
  98.2 49.6 %collective-permute-start = (bf16[14,128,512]{2,1,0:T(8,128)(2,1)}, bf16[14,128,512]{2,1,0:T(8,128)(2,1)}, u32[]{:S(2)}, u32[]{:S(2)}) collective-permute-start(bf16[14,128,512]{2,1,0:T(8,128)(2,1)} %convolution_convert_fusion), channel_id=1, source_target_pairs={{0,3},{1,0},{2,1},{3,2},{4,7},{5,4},{6,5},{7,6},{8,11},{9,8},{10,9... | collective-permute-start | bytes 5505032 | tf_op jit(solution)/shard_map/ppermute | solution.py:53
  98.4 51.7 %collective-permute-start.2 = (bf16[14,128,512]{2,1,0:T(8,128)(2,1)}, bf16[14,128,512]{2,1,0:T(8,128)(2,1)}, u32[]{:S(2)}, u32[]{:S(2)}) collective-permute-start(bf16[14,128,512]{2,1,0:T(8,128)(2,1)} %collective-permute-done.1), channel_id=1, source_target_pairs={{0,1},{1,2},{2,3},{3,0},{4,5},{5,6},{6,7},{7,4},{8,9},{9,10},{10,1... | collective-permute-start | bytes 5505032 | tf_op jit(solution)/shard_map/ppermute | solution.py:51
  147.7 2.3 copy-start.1
  160.2 0.7 copy-start.5
  160.2 19.5 %copy-start.7 = (u32[32]{0:T(128)S(1)}, u32[32]{0:T(128)}, u32[]{:S(2)}) copy-start(u32[32]{0:T(128)} %constant.85) | copy-start | bytes 388
  160.2 22.0 %copy-start.4 = (bf16[14,512]{1,0:T(8,128)(2,1)S(1)}, bf16[14,512]{1,0:T(8,128)(2,1)}, u32[]{:S(2)}) copy-start(bf16[14,512]{1,0:T(8,128)(2,1)} %param.12) | copy-start | bytes 43012
  160.2 137.6 %reduce-scatter.5.cloned.1.call-start = ((), (), s32[]{:S(2)}) async-start(), calls=%async_computation.4 | async-start | bytes 40960 | tf_op jit(solution)/shard_map/reduce_scatter | solution.py:82
  179.7 2.5 copy-start.2
Sparse Core Ops, SparseCore 0:
  10.4 55.0 all-gather.4
  160.3 108.7 reduce-scatter.2
  278.2 19.5 reduce-scatter.4
Sparse Core Ops, SparseCore 1:
  98.2 40.3 all-gather.6
